TPU v7x, 256 devices: a whole 4x4x8 slice. The times are simulated.
256 devices in a mesh: gx: 8 (over y, core), gy: 8 (over z), ba: 4 (over x).
Axes of the slice: x: 4, y: 4, z: 8, core: 2. Of those that a mesh axis runs over, the one named last changes fastest.
Arguments:
- pixels: float32 [224, 128, 1024], P('ba', 'gy', 'gx'), may hold values from -8 to 8
- spectra: float32 [224, 256], P('ba'), may hold values from -0.375 to 0.375
- abundance: float32 [256, 128, 1024], P('ba', 'gy', 'gx'), may hold values from 0 to 1
- plan: int32 [3], replicated, may hold values from 0 to 1, as said below
Outputs:
- sparse: float32 [256, 128, 1024], P('ba', 'gy', 'gx')
- spectra_grad: float32 [224, 256], P('ba')
Inputs may be any that keep to these rules, and one draw needn't show every extreme that they name: `plan`: entry 0 is 1 and at least one later entry is 0.
All inputs are finite; a program needn't handle non-finite values. Where the computation divides by a largest or mean magnitude, that divisor is 1e-20 or more.
Results may differ from a plain program's by a relative error of at most 0.0001.
Values sent between devices are 32-bit elements; how exact they have to be, the bound alone decides.
No kernel may reach another device: no remote copies, remote signals or barrier semaphores. Data moves between devices by JAX's collectives and lax.ppermute only.
A program may use at most 64 MiB of HBM per device.

v0:
```python
import math
import jax
import jax.numpy as jnp
from jax import lax
from jax.sharding import PartitionSpec as P

SWEEPS = 3
HIGHEST = lax.Precision.HIGHEST
penalty = 1.0
tv_weight = 0.2
sparsity = 0.05


def extended_2(x, sides, width):
    for axis, dim in sides:
        size, length = (lax.axis_size(axis), x.shape[dim])
        up = [(i, (i + 1) % size) for i in range(size - 1)]
        down = [(j, i) for i, j in up]
        last = lax.slice_in_dim(x, length - width, length, axis=dim)
        leading = lax.slice_in_dim(x, 0, width, axis=dim)
        before = lax.ppermute(last, axis, up)
        after = lax.ppermute(leading, axis, down)
        x = jnp.concatenate([before, x, after], axis=dim)
    return x


def edge_masks(top_row, left_col, row_count, col_count, grid_rows, grid_cols):
    ext_rows = top_row - 1 + jnp.arange(row_count + 1)
    ext_cols = left_col - 1 + jnp.arange(col_count + 1)
    rows_in = (ext_rows >= 0) & (ext_rows <= grid_rows - 1)
    cols_in = (ext_cols >= 0) & (ext_cols <= grid_cols - 1)
    rows_ok = (ext_rows >= 0) & (ext_rows <= grid_rows - 2)
    cols_ok = (ext_cols >= 0) & (ext_cols <= grid_cols - 2)
    mask_h = (rows_in[:, None] & cols_ok[None, :]).astype(jnp.float32)[None]
    mask_v = (rows_ok[:, None] & cols_in[None, :]).astype(jnp.float32)[None]
    return (mask_h, mask_v)


def local(pixels, spectra, abundance, plan):
    comp_share, row_count, gx_cols = abundance.shape
    band_ways = lax.axis_size("ba")
    grid_rows = row_count * lax.axis_size("gy")
    grid_cols = gx_cols * lax.axis_size("gx")
    all_comps = comp_share * band_ways
    top_row = lax.axis_index("gy") * row_count
    all_spectra = lax.all_gather(spectra, "ba", axis=0, tiled=True)
    first_comp = lax.axis_index("ba") * comp_share
    own_cols = lax.dynamic_slice_in_dim(all_spectra, first_comp, comp_share, 1)
    gram_rows = jnp.dot(own_cols.T, all_spectra, precision=HIGHEST)
    bound = lax.pmax(jnp.max(jnp.sum(jnp.abs(gram_rows), axis=1)), "ba")
    left_col = lax.axis_index("gx") * gx_cols
    mask_h, mask_v = edge_masks(top_row, left_col, row_count, gx_cols, grid_rows, grid_cols)
    field = abundance
    sparse = abundance
    dual = jnp.zeros_like(abundance)
    weight = jnp.ones((comp_share, row_count + 1, gx_cols + 1), jnp.float32)
    for sweep in range(SWEEPS):
        extended = extended_2(field, (("gx", 2), ("gy", 1)), 1)
        center = extended[:, : row_count + 1, : gx_cols + 1]
        right = extended[:, : row_count + 1, 1:]
        below = extended[:, 1:, : gx_cols + 1]
        diff_h = (right - center) * mask_h
        diff_v = (below - center) * mask_v
        energy = diff_h * diff_h + diff_v * diff_v
        total = lax.psum(jnp.sum(energy[:, 1:, 1:]), ("gx", "gy", "ba"))
        smooth_sq = total / (all_comps * grid_rows * grid_cols) + 1e-06
        fresh = 1.0 / jnp.sqrt(energy + smooth_sq)
        weight = jnp.where(plan[sweep] == 1, fresh, weight)
        flux_h = weight * diff_h
        flux_v = weight * diff_v
        edge_h = weight * mask_h
        edge_v = weight * mask_v
        tv_grad = flux_h[:, 1:, :-1] - flux_h[:, 1:, 1:] + flux_v[:, :-1, 1:] - flux_v[:, 1:, 1:]
        degree = edge_h[:, 1:, 1:] + edge_h[:, 1:, :-1] + edge_v[:, 1:, 1:] + edge_v[:, :-1, 1:]
        mixed = jnp.einsum(
            "lq,qrc->lrc",
            spectra,
            lax.all_gather(field, "ba", axis=0, tiled=True),
            precision=HIGHEST,
        )
        resid = mixed - pixels
        data_grad = lax.psum_scatter(
            jnp.einsum("lp,lrc->prc", spectra, resid, precision=HIGHEST),
            "ba",
            scatter_dimension=0,
            tiled=True,
        )
        grad_total = data_grad + tv_weight * tv_grad + penalty * (field - sparse + dual)
        field = field - grad_total / (bound + penalty + 2.0 * tv_weight * degree)
        sparse = jnp.maximum(field + dual - sparsity / penalty, 0.0)
        dual = dual + field - sparse
    all_sparse = lax.all_gather(sparse, "ba", axis=0, tiled=True)
    resid = jnp.einsum("lp,prc->lrc", spectra, all_sparse, precision=HIGHEST) - pixels
    partial_grad = jnp.einsum("lrc,prc->lp", resid, all_sparse, precision=HIGHEST) / math.sqrt(
        grid_rows * grid_cols
    )
    spectra_grad = lax.psum(partial_grad, ("gx", "gy"))
    return (sparse, spectra_grad)


def solution(mesh):
    return jax.shard_map(
        local,
        mesh=mesh,
        in_specs=(P("ba", "gy", "gx"), P("ba", None), P("ba", "gy", "gx"), P()),
        out_specs=(P("ba", "gy", "gx"), P("ba", None)),
        check_vma=False,
    )
```

profile of v0, /device:TPU:2, one launch (start us, length us, event | category | flops | bytes accessed | tf_op | source)
XLA Modules:
  0.0 793.5 jit_solution(9205692723680209742)
XLA Ops:
  7.2 0.7 all-gather.5.cloned.1.call-update
  8.0 37.2 %all-gather.5.cloned.1.call-done = f32[256,16,128]{2,1,0:T(8,128)} async-done(((f32[64,16,128]{2,1,0:T(8,128)}), f32[256,16,128]{2,1,0:T(8,128)}) %all-gather.5.cloned.1.call-update) | async-done | bytes 2097168 | tf_op jit(solution)/shard_map/all_gather | solution.py:78
  45.1 3.5 fusion.4
  48.8 1.8 convolution_bitcast_fusion.2
  50.6 2.0 copy.19
  52.7 1.0 copy-done.2
  53.9 1.6 collective-permute-start
  55.5 1.3 collective-permute-start.1
  56.8 12.2 %all_gather.16 = f32[224,256]{1,0:T(8,128)S(1)} all-gather(f32[56,256]{1,0:T(8,128)S(1)} %copy-done.14), channel_id=1, replica_groups=mesh['gx'=8,'gy'=8,'ba'=4] {'ba'}, dimensions={0}, use_global_device_ids=true | all-gather | bytes 286720 | tf_op jit(solution)/shard_map/all_gather | solution.py:46
  70.8 3.5 collective-permute-start.2
  74.2 0.7 fusion.73
  74.9 10.9 %pmax.7 = f32[]{:T(128)} all-reduce(f32[]{:T(128)} %reduce_max.9), channel_id=1, replica_groups=mesh['gx'=8,'gy'=8,'ba'=4] {'ba'}, use_global_device_ids=true, to_apply=%region_5.6 | all-reduce | flops 1 | bytes 8 | tf_op jit(solution)/shard_map/pmax | solution.py:50
  86.5 1.3 collective-permute-start.3
  87.8 0.7 maximum_maximum_fusion
  88.5 4.2 collective-permute-done.3
  92.6 0.9 multiply_add_fusion.2
  93.5 1.1 copy-done.3
  94.7 0.8 slice_reduce_fusion.2
  96.1 78.7 %psum.28 = f32[]{:T(128)} all-reduce(f32[]{:T(128)} %slice_reduce_fusion.2), channel_id=1, replica_groups=mesh['gx'=8,'gy'=8,'ba'=4] {'gx','gy','ba'}, use_global_device_ids=true, to_apply=%region_2.0 | all-reduce | flops 1 | bytes 8 | tf_op jit(solution)/shard_map/psum | solution.py:65
  175.5 5.1 fusion.55
  180.6 6.1 fusion.45
  187.0 30.1 %all-gather.7.cloned.1.call-done = f32[256,16,128]{2,1,0:T(8,128)} async-done(((f32[64,16,128]{2,1,0:T(8,128)}), f32[256,16,128]{2,1,0:T(8,128)}) %all-gather.7.cloned.1.call-update) | async-done | bytes 2097168 | tf_op jit(solution)/shard_map/all_gather | solution.py:78
  217.1 3.5 fusion.2
  220.8 1.8 convolution_bitcast_fusion.1
  222.6 2.0 copy.21
  224.7 1.0 copy-done
  225.8 1.6 collective-permute-start.4
  227.4 1.3 collective-permute-start.5
  228.9 3.7 collective-permute-done.5
  233.1 3.5 collective-permute-start.6
  236.6 1.3 collective-permute-start.7
  238.5 0.7 maximum_maximum_fusion.1
  239.2 3.6 collective-permute-done.7
  242.8 0.9 multiply_add_fusion.1
  243.7 1.2 copy-done.6
  244.8 0.8 slice_reduce_fusion.1
  246.3 83.2 %psum.29 = f32[]{:T(128)} all-reduce(f32[]{:T(128)} %slice_reduce_fusion.1), channel_id=1, replica_groups=mesh['gx'=8,'gy'=8,'ba'=4] {'gx','gy','ba'}, use_global_device_ids=true, to_apply=%region_8.9 | all-reduce | flops 1 | bytes 8 | tf_op jit(solution)/shard_map/psum | solution.py:65
  330.1 3.6 fusion.56
  333.8 1.1 copy-done.4
  334.9 2.7 fusion.68
  337.6 6.1 fusion.38
  344.0 29.8 %all-gather.9.cloned.1.call-done = f32[256,16,128]{2,1,0:T(8,128)} async-done(((f32[64,16,128]{2,1,0:T(8,128)}), f32[256,16,128]{2,1,0:T(8,128)}) %all-gather.9.cloned.1.call-update) | async-done | bytes 2097168 | tf_op jit(solution)/shard_map/all_gather | solution.py:78
  373.8 3.5 fusion
  377.5 1.8 convolution_bitcast_fusion
  379.3 2.0 copy.23
  381.4 1.0 copy-done.1
  382.5 1.6 collective-permute-start.8
  384.1 1.3 collective-permute-start.9
  385.6 3.7 collective-permute-done.9
  389.8 3.5 collective-permute-start.10
  393.3 1.3 collective-permute-start.11
  395.2 0.7 maximum_maximum_fusion.2
  395.9 3.6 collective-permute-done.11
  399.5 0.9 multiply_add_fusion
  400.4 1.2 copy-done.5
  401.5 0.8 slice_reduce_fusion
  403.0 83.4 %psum.30 = f32[]{:T(128)} all-reduce(f32[]{:T(128)} %slice_reduce_fusion), channel_id=1, replica_groups=mesh['gx'=8,'gy'=8,'ba'=4] {'gx','gy','ba'}, use_global_device_ids=true, to_apply=%region_11.12 | all-reduce | flops 1 | bytes 8 | tf_op jit(solution)/shard_map/psum | solution.py:65
  487.1 3.7 fusion.57
  490.8 2.6 fusion.69
  493.4 6.1 fusion.49
  499.6 30.1 %all-gather.11.cloned.1.call-done = f32[256,16,128]{2,1,0:T(8,128)} async-done(((f32[64,16,128]{2,1,0:T(8,128)}), f32[256,16,128]{2,1,0:T(8,128)}) %all-gather.11.cloned.1.call-update) | async-done | bytes 2097168 | tf_op jit(solution)/shard_map/all_gather | solution.py:92
  529.7 3.7 fusion.6
  533.5 2.3 fusion.22
  535.8 250.9 %psum.31 = f32[56,256]{1,0:T(8,128)} all-reduce(f32[56,256]{1,0:T(8,128)S(1)} %fusion.22), channel_id=1, replica_groups=mesh['gx'=8,'gy'=8,'ba'=4] {'gx','gy'}, use_global_device_ids=true, to_apply=%region_12.13 | all-reduce | flops 14336 | bytes 114688 | tf_op jit(solution)/shard_map/psum | solution.py:97
  (64 shorter events, 6.2 us)
Async XLA Ops:
  7.2 41.5 %copy-start.10 = (f32[56,16,128]{2,1,0:T(8,128)S(1)}, f32[56,16,128]{2,1,0:T(8,128)}, u32[]{:S(2)}) copy-start(f32[56,16,128]{2,1,0:T(8,128)} %param.4) | copy-start | bytes 1376260
  7.2 38.0 %all-gather.5.cloned.1.call-start = ((), (), s32[]{:S(2)}) async-start(), calls=%async_computation.3 | async-start | bytes 2621440 | tf_op jit(solution)/shard_map/all_gather | solution.py:78
  7.9 40.9 %copy-start.14 = (f32[56,256]{1,0:T(8,128)S(1)}, f32[56,256]{1,0:T(8,128)}, u32[]{:S(2)}) copy-start(f32[56,256]{1,0:T(8,128)} %param.5) | copy-start | bytes 172036
  7.9 172.7 %reduce-scatter.4.cloned.1.call-start = ((), (), s32[]{:S(2)}) async-start(), calls=%async_computation.4 | async-start | bytes 2621440 | tf_op jit(solution)/shard_map/reduce_scatter | solution.py:82
  52.6 1.0 copy-start.2
  52.6 164.5 %all-gather.7.cloned.1.call-start = ((), (), s32[]{:S(2)}) async-start(), calls=%async_computation.5 | async-start | bytes 2621440 | tf_op jit(solution)/shard_map/all_gather | solution.py:78
  53.9 20.4 %copy-start.15 = (s32[3]{0:T(128)S(1)}, s32[3]{0:T(128)}, u32[]{:S(2)}) copy-start(s32[3]{0:T(128)} %param.7) | copy-start | bytes 40
  53.9 16.4 %collective-permute-start = (f32[64,16,1]{2,1,0:T(8,128)S(1)}, f32[64,16,1]{2,1,0:T(8,128)S(1)}, u32[]{:S(2)}, u32[]{:S(2)}) collective-permute-start(f32[64,16,1]{2,1,0:T(8,128)S(1)} %get-tuple-element.28), channel_id=1, source_target_pairs={{0,32},{32,64},{64,96},{96,128},{128,160},{160,192},{192,224},{1,3... | collective-permute-start | bytes 12296 | tf_op jit(solution)/shard_map/ppermute | solution.py:21
  55.5 14.8 %collective-permute-start.1 = (f32[64,16,1]{2,1,0:T(8,128)S(1)}, f32[64,16,1]{2,1,0:T(8,128)S(1)}, u32[]{:S(2)}, u32[]{:S(2)}) collective-permute-start(f32[64,16,1]{2,1,0:T(8,128)S(1)} %get-tuple-element.29), channel_id=1, source_target_pairs={{32,0},{64,32},{96,64},{128,96},{160,128},{192,160},{224,192},{33,... | collective-permute-start | bytes 12296 | tf_op jit(solution)/shard_map/ppermute | solution.py:22
  70.8 17.0 %collective-permute-start.2 = (f32[64,1,130]{2,1,0:T(1,128)S(1)}, f32[64,1,130]{2,1,0:T(1,128)S(1)}, u32[]{:S(2)}, u32[]{:S(2)}) collective-permute-start(f32[64,1,130]{2,1,0:T(1,128)S(1)} %get-tuple-element.23), channel_id=1, source_target_pairs={{0,4},{4,8},{8,12},{12,16},{16,20},{20,24},{24,28},{1,5},{5,9},{9,... | collective-permute-start | bytes 99848 | tf_op jit(solution)/shard_map/ppermute | solution.py:21
  86.5 6.2 collective-permute-start.3
  93.5 1.1 copy-start.3
  186.7 33.9 %copy-start.11 = (f32[56,16,128]{2,1,0:T(8,128)S(1)}, f32[56,16,128]{2,1,0:T(8,128)}, u32[]{:S(2)}) copy-start(f32[56,16,128]{2,1,0:T(8,128)} %param.4) | copy-start | bytes 1376260
  186.7 150.9 %reduce-scatter.6.cloned.1.call-start = ((), (), s32[]{:S(2)}) async-start(), calls=%async_computation.6 | async-start | bytes 2621440 | tf_op jit(solution)/shard_map/reduce_scatter | solution.py:82
  224.6 1.0 copy-start
  224.6 149.2 %all-gather.9.cloned.1.call-start = ((), (), s32[]{:S(2)}) async-start(), calls=%async_computation.7 | async-start | bytes 2621440 | tf_op jit(solution)/shard_map/all_gather | solution.py:78
  225.8 3.1 collective-permute-start.4
  227.4 5.2 collective-permute-start.5
  233.1 5.3 collective-permute-start.6
  236.6 6.2 collective-permute-start.7
  243.7 1.2 copy-start.6
  333.8 1.1 copy-start.4
  343.7 33.6 %copy-start.12 = (f32[56,16,128]{2,1,0:T(8,128)S(1)}, f32[56,16,128]{2,1,0:T(8,128)}, u32[]{:S(2)}) copy-start(f32[56,16,128]{2,1,0:T(8,128)} %param.4) | copy-start | bytes 1376260
  343.7 149.7 %reduce-scatter.8.cloned.1.call-start = ((), (), s32[]{:S(2)}) async-start(), calls=%async_computation.8 | async-start | bytes 2621440 | tf_op jit(solution)/shard_map/reduce_scatter | solution.py:82
  381.3 1.0 copy-start.1
  381.3 148.3 %all-gather.11.cloned.1.call-start = ((), (), s32[]{:S(2)}) async-start(), calls=%async_computation.9 | async-start | bytes 2621440 | tf_op jit(solution)/shard_map/all_gather | solution.py:92
  382.5 3.1 collective-permute-start.8
  384.1 5.2 collective-permute-start.9
  389.3 10.1 %copy-start.7 = (f32[64,16,1]{2,1,0:T(8,128)}, f32[64,16,1]{2,1,0:T(8,128)S(1)}, u32[]{:S(2)}) copy-start(f32[64,16,1]{2,1,0:T(8,128)S(1)} %collective-permute-done.9) | copy-start | bytes 12292
  389.8 5.3 collective-permute-start.10
  393.3 6.2 collective-permute-start.11
  400.4 1.2 copy-start.5
  487.1 3.7 copy-start.8
  499.6 33.8 %copy-start.13 = (f32[56,16,128]{2,1,0:T(8,128)S(1)}, f32[56,16,128]{2,1,0:T(8,128)}, u32[]{:S(2)}) copy-start(f32[56,16,128]{2,1,0:T(8,128)} %param.4) | copy-start | bytes 1376260
  529.6 3.8 copy-start.9
Sparse Core Ops, SparseCore 0:
  9.8 35.2 all-gather.4
  52.8 32.7 reduce-scatter.3
  186.9 30.1 all-gather.6
  224.7 31.9 reduce-scatter.5
  343.9 29.8 all-gather.8
  381.4 31.9 reduce-scatter.7
  499.7 29.8 all-gather.10
where the time goes:
time: 795 us; the launch traced here: 794 us
  blocking collectives  519 us (65%)
  waiting for transfers between devices  148 us (19%)
  other arithmetic  46 us (6%)
  starting transfers between devices  23.6 us (3%)
  matrix products  22.7 us (3%)
  between operations  19.1 us (2%)
  local copies, waits for them, and re-layouts  14.7 us (2%)
    psum x1, blocking collectives, local(): spectra_grad = lax.psum(partial_grad, ('gx', 'gy'))  251 us
    psum x3, blocking collectives, local(): total = lax.psum(jnp.sum(energy[:, 1:, 1:]), ('gx', 'gy', 'ba'))  245 us
    all_gather x3, waiting for transfers between devices, local(): lax.all_gather(field, 'ba', axis=0, tiled=True)  97.1 us
    all_gather x1, waiting for transfers between devices, local(): all_sparse = lax.all_gather(sparse, 'ba', axis=0, tiled=True)  30.1 us
    ppermute x6, waiting for transfers between devices, extended_2(): after = lax.ppermute(leading, axis, down)  18.8 us
  transfers between devices with their start and end apart: 19, of which 13 were waited for; matrix products, arithmetic and copies ran while one was open for 4% of the time, Pallas kernels for 0%

commit v1 on v0

--- a/solution.py
+++ b/solution.py
@@ -72,11 +72,37 @@
         edge_v = weight * mask_v
         tv_grad = flux_h[:, 1:, :-1] - flux_h[:, 1:, 1:] + flux_v[:, :-1, 1:] - flux_v[:, 1:, 1:]
         degree = edge_h[:, 1:, 1:] + edge_h[:, 1:, :-1] + edge_v[:, 1:, 1:] + edge_v[:, :-1, 1:]
-        mixed = jnp.einsum(
-            "lq,qrc->lrc",
-            spectra,
-            lax.all_gather(field, "ba", axis=0, tiled=True),
-            precision=HIGHEST,
+
+        def _bind_lane(s0, which_axis, body):
+            vec_out = lax.axis_size(which_axis)
+            carry = lax.axis_index(which_axis)
+            formed, piece_now, small = (vec_out, carry, s0.shape[0])
+            main = range(formed)
+            opened = map(lambda dev: (dev, (dev + 1) % formed), main)
+            by_rank = list(map(lambda dev: (dev, (dev - 1) % formed), range(formed)))
+            back = formed // 2
+            t1 = then = s0
+            work_now = body(s0, piece_now * small)
+            in_order = list(opened)
+            for nth in range(1, back + 1):
+                t1 = lax.ppermute(t1, which_axis, in_order)
+                if nth < formed - back:
+                    then = lax.ppermute(then, which_axis, by_rank)
+                    block_last = body(then, (piece_now + nth) % formed * small)
+                    work_now = work_now + block_last
+                seen_now = body(t1, (piece_now - nth) % formed * small)
+                work_now = work_now + seen_now
+            return work_now
+
+        mixed = _bind_lane(
+            field,
+            "ba",
+            lambda own_block, at: jnp.einsum(
+                "lq,qrc->lrc",
+                lax.dynamic_slice_in_dim(spectra, at, own_block.shape[0], axis=1),
+                own_block,
+                precision=HIGHEST,
+            ),
         )
         resid = mixed - pixels
         data_grad = lax.psum_scatter(

time: 795 us -> 776 us (0.976)
  waiting for transfers between devices: 148 us -> 112 us
    all_gather x3 -> x0, waiting for transfers between devices: 97.1 us -> none  [local(): lax.all_gather(field, 'ba', axis=0, tiled=True)]
    ppermute x0 -> x9, waiting for transfers between devices: none -> 63.3 us  [the longest x6 63.3 us: _bind_lane(): t1 = lax.ppermute(t1, which_axis, in_order)]
    ppermute x0 -> x9, starting transfers between devices: none -> 10.9 us  [the longest x6 7.72 us: _bind_lane(): t1 = lax.ppermute(t1, which_axis, in_order)]
  transfers between devices with their start and end apart: 19 -> 25, of which waited for: 13 -> 16; matrix products, arithmetic and copies ran while one was open for 4% -> 5% of each run, Pallas kernels for 0% -> 0%
where the time goes in v1:
time: 776 us; the launch traced here: 767 us
  blocking collectives  525 us (68%)
  waiting for transfers between devices  112 us (14%)
  other arithmetic  44.8 us (6%)
  starting transfers between devices  29.6 us (4%)
  matrix products  23.2 us (3%)
  between operations  19.3 us (2%)
  local copies, waits for them, and re-layouts  12.8 us (2%)
    psum x1, blocking collectives, local(): spectra_grad = lax.psum(partial_grad, ('gx', 'gy'))  251 us
    psum x3, blocking collectives, local(): total = lax.psum(jnp.sum(energy[:, 1:, 1:]), ('gx', 'gy', 'ba'))  250 us
    ppermute x6, waiting for transfers between devices, _bind_lane(): t1 = lax.ppermute(t1, which_axis, in_order)  63.3 us
    all_gather x1, waiting for transfers between devices, local(): all_sparse = lax.all_gather(sparse, 'ba', axis=0, tiled=True)  30.1 us
    ppermute x6, waiting for transfers between devices, extended_2(): after = lax.ppermute(leading, axis, down)  17.2 us
  transfers between devices with their start and end apart: 25, of which 16 were waited for; matrix products, arithmetic and copies ran while one was open for 5% of the time, Pallas kernels for 0%

profile of v1, /device:TPU:2, one launch (start us, length us, event | category | flops | bytes accessed | tf_op | source)
XLA Modules:
  0.0 767.0 jit_solution(17329723712737660331)
XLA Ops:
  7.2 1.6 collective-permute-start.1
  8.8 0.8 collective-permute-start
  9.6 11.5 %collective-permute-done.1 = f32[64,16,128]{2,1,0:T(8,128)S(1)} collective-permute-done((f32[64,16,128]{2,1,0:T(8,128)}, f32[64,16,128]{2,1,0:T(8,128)S(1)}, u32[]{:S(2)}, u32[]{:S(2)}) %collective-permute-start.1) | collective-permute-done | bytes 524320 | tf_op jit(solution)/shard_map/ppermute | solution.py:88
  21.2 1.5 collective-permute-start.2
  22.7 1.7 fusion.65
  24.5 1.5 fusion.61
  26.7 7.2 collective-permute-done.2
  33.9 1.7 fusion.59
  35.9 1.8 convolution_bitcast_fusion.2
  37.7 2.0 copy.19
  39.8 1.0 copy-done
  41.0 1.3 collective-permute-start.3
  42.3 1.3 collective-permute-start.4
  43.6 13.4 %all_gather.6 = f32[224,256]{1,0:T(8,128)S(1)} all-gather(f32[56,256]{1,0:T(8,128)S(1)} %copy-done.12), channel_id=1, replica_groups=mesh['gx'=8,'gy'=8,'ba'=4] {'ba'}, dimensions={0}, use_global_device_ids=true | all-gather | bytes 286720 | tf_op jit(solution)/shard_map/all_gather | solution.py:46
  58.9 3.6 collective-permute-start.5
  63.1 11.3 %pmax.7 = f32[]{:T(128)} all-reduce(f32[]{:T(128)} %reduce_max.9), channel_id=1, replica_groups=mesh['gx'=8,'gy'=8,'ba'=4] {'ba'}, use_global_device_ids=true, to_apply=%region_5.6 | all-reduce | flops 1 | bytes 8 | tf_op jit(solution)/shard_map/pmax | solution.py:50
  75.1 1.3 collective-permute-start.6
  77.1 4.2 collective-permute-done.6
  81.3 0.9 multiply_add_fusion.2
  82.2 1.1 copy-done.1
  84.8 80.8 %psum.28 = f32[]{:T(128)} all-reduce(f32[]{:T(128)} %slice_reduce_fusion.2), channel_id=1, replica_groups=mesh['gx'=8,'gy'=8,'ba'=4] {'gx','gy','ba'}, use_global_device_ids=true, to_apply=%region_2.0 | all-reduce | flops 1 | bytes 8 | tf_op jit(solution)/shard_map/psum | solution.py:65
  166.2 5.1 fusion.76
  171.3 5.3 fusion.39
  177.4 1.4 collective-permute-start.7
  178.8 11.7 %collective-permute-done.8 = f32[64,16,128]{2,1,0:T(8,128)S(1)} collective-permute-done((f32[64,16,128]{2,1,0:T(8,128)S(1)}, f32[64,16,128]{2,1,0:T(8,128)S(1)}, u32[]{:S(2)}, u32[]{:S(2)}) %collective-permute-start.8) | collective-permute-done | bytes 524320 | tf_op jit(solution)/shard_map/ppermute | solution.py:88
  193.2 10.8 %collective-permute-done.9 = f32[64,16,128]{2,1,0:T(8,128)S(1)} collective-permute-done((f32[64,16,128]{2,1,0:T(8,128)S(1)}, f32[64,16,128]{2,1,0:T(8,128)S(1)}, u32[]{:S(2)}, u32[]{:S(2)}) %collective-permute-start.9) | collective-permute-done | bytes 524320 | tf_op jit(solution)/shard_map/ppermute | solution.py:88
  205.0 1.8 convolution_bitcast_fusion.1
  206.8 2.0 copy.21
  209.1 1.3 collective-permute-start.10
  210.4 1.3 collective-permute-start.11
  211.9 3.3 collective-permute-done.11
  215.7 1.7 collective-permute-start.12
  217.5 1.5 collective-permute-start.13
  220.0 3.6 collective-permute-done.13
  223.6 0.9 multiply_add_fusion.1
  224.5 1.2 copy-done.4
  227.2 83.9 %psum.29 = f32[]{:T(128)} all-reduce(f32[]{:T(128)} %slice_reduce_fusion.1), channel_id=1, replica_groups=mesh['gx'=8,'gy'=8,'ba'=4] {'gx','gy','ba'}, use_global_device_ids=true, to_apply=%region_8.9 | all-reduce | flops 1 | bytes 8 | tf_op jit(solution)/shard_map/psum | solution.py:65
  311.7 3.6 fusion.77
  315.3 1.1 copy-done.2
  316.4 2.7 fusion.122
  319.1 5.3 fusion.32
  324.5 1.9 collective-permute-start.15
  326.4 1.0 collective-permute-start.14
  327.3 11.6 %collective-permute-done.15 = f32[64,16,128]{2,1,0:T(8,128)S(1)} collective-permute-done((f32[64,16,128]{2,1,0:T(8,128)S(1)}, f32[64,16,128]{2,1,0:T(8,128)S(1)}, u32[]{:S(2)}, u32[]{:S(2)}) %collective-permute-start.15) | collective-permute-done | bytes 524320 | tf_op jit(solution)/shard_map/ppermute | solution.py:88
  338.9 1.4 collective-permute-start.16
  342.4 10.5 %collective-permute-done.16 = f32[64,16,128]{2,1,0:T(8,128)S(1)} collective-permute-done((f32[64,16,128]{2,1,0:T(8,128)S(1)}, f32[64,16,128]{2,1,0:T(8,128)S(1)}, u32[]{:S(2)}, u32[]{:S(2)}) %collective-permute-start.16) | collective-permute-done | bytes 524320 | tf_op jit(solution)/shard_map/ppermute | solution.py:88
  353.9 1.8 convolution_bitcast_fusion
  355.8 2.0 copy.23
  358.0 1.3 collective-permute-start.17
  359.3 1.3 collective-permute-start.18
  360.8 2.5 collective-permute-done.18
  363.8 1.3 collective-permute-start.19
  365.1 1.3 collective-permute-start.20
  367.7 3.6 collective-permute-done.20
  371.2 0.9 multiply_add_fusion
  372.2 1.2 copy-done.3
  374.8 85.1 %psum.30 = f32[]{:T(128)} all-reduce(f32[]{:T(128)} %slice_reduce_fusion), channel_id=1, replica_groups=mesh['gx'=8,'gy'=8,'ba'=4] {'gx','gy','ba'}, use_global_device_ids=true, to_apply=%region_11.12 | all-reduce | flops 1 | bytes 8 | tf_op jit(solution)/shard_map/psum | solution.py:65
  460.5 3.7 fusion.78
  464.2 2.6 fusion.123
  466.8 6.0 fusion.67
  472.8 30.1 %all-gather.2.cloned.1.call-done = f32[256,16,128]{2,1,0:T(8,128)} async-done(((f32[64,16,128]{2,1,0:T(8,128)}), f32[256,16,128]{2,1,0:T(8,128)}) %all-gather.2.cloned.1.call-update) | async-done | bytes 2097168 | tf_op jit(solution)/shard_map/all_gather | solution.py:118
  503.0 3.7 fusion
  506.8 2.3 fusion.16
  509.1 250.9 %psum.31 = f32[56,256]{1,0:T(8,128)} all-reduce(f32[56,256]{1,0:T(8,128)S(1)} %fusion.16), channel_id=1, replica_groups=mesh['gx'=8,'gy'=8,'ba'=4] {'gx','gy'}, use_global_device_ids=true, to_apply=%region_12.13 | all-reduce | flops 14336 | bytes 114688 | tf_op jit(solution)/shard_map/psum | solution.py:123
  (78 shorter events, 18.7 us)
Async XLA Ops:
  7.2 18.8 %copy-start.12 = (f32[56,256]{1,0:T(8,128)S(1)}, f32[56,256]{1,0:T(8,128)}, u32[]{:S(2)}) copy-start(f32[56,256]{1,0:T(8,128)} %param.5) | copy-start | bytes 172036
  7.2 164.2 %reduce-scatter.4.cloned.1.call-start = ((), (), s32[]{:S(2)}) async-start(), calls=%async_computation.3 | async-start | bytes 2621440 | tf_op jit(solution)/shard_map/reduce_scatter | solution.py:108
  7.2 14.0 %collective-permute-start.1 = (f32[64,16,128]{2,1,0:T(8,128)}, f32[64,16,128]{2,1,0:T(8,128)S(1)}, u32[]{:S(2)}, u32[]{:S(2)}) collective-permute-start(f32[64,16,128]{2,1,0:T(8,128)} %param.6), channel_id=1, source_target_pairs={{0,1},{1,2},{2,3},{3,0},{4,5},{5,6},{6,7},{7,4},{8,9},{9,10},{10,1... | collective-permute-start | bytes 1572872 | tf_op jit(solution)/shard_map/ppermute | solution.py:88
  8.8 17.2 %collective-permute-start = (f32[64,16,128]{2,1,0:T(8,128)}, f32[64,16,128]{2,1,0:T(8,128)S(1)}, u32[]{:S(2)}, u32[]{:S(2)}) collective-permute-start(f32[64,16,128]{2,1,0:T(8,128)} %param.6), channel_id=1, source_target_pairs={{0,3},{1,0},{2,1},{3,2},{4,7},{5,4},{6,5},{7,6},{8,11},{9,8},{10,9... | collective-permute-start | bytes 1572872 | tf_op jit(solution)/shard_map/ppermute | solution.py:90
  21.2 12.7 %collective-permute-start.2 = (f32[64,16,128]{2,1,0:T(8,128)S(1)}, f32[64,16,128]{2,1,0:T(8,128)}, u32[]{:S(2)}, u32[]{:S(2)}) collective-permute-start(f32[64,16,128]{2,1,0:T(8,128)S(1)} %collective-permute-done.1), channel_id=1, source_target_pairs={{0,1},{1,2},{2,3},{3,0},{4,5},{5,6},{6,7},{7,4},{8,9},{9,10},{10,1... | collective-permute-start | bytes 1572872 | tf_op jit(solution)/shard_map/ppermute | solution.py:88
  24.4 11.2 %copy-start.8 = (f32[56,16,128]{2,1,0:T(8,128)S(1)}, f32[56,16,128]{2,1,0:T(8,128)}, u32[]{:S(2)}) copy-start(f32[56,16,128]{2,1,0:T(8,128)} %param.4) | copy-start | bytes 1376260
  39.7 1.0 copy-start
  39.7 279.4 %reduce-scatter.6.cloned.1.call-start = ((), (), s32[]{:S(2)}) async-start(), calls=%async_computation.4 | async-start | bytes 2621440 | tf_op jit(solution)/shard_map/reduce_scatter | solution.py:108
  41.0 21.5 %copy-start.13 = (s32[3]{0:T(128)S(1)}, s32[3]{0:T(128)}, u32[]{:S(2)}) copy-start(s32[3]{0:T(128)} %param.7) | copy-start | bytes 40
  41.0 17.4 %collective-permute-start.3 = (f32[64,16,1]{2,1,0:T(8,128)S(1)}, f32[64,16,1]{2,1,0:T(8,128)S(1)}, u32[]{:S(2)}, u32[]{:S(2)}) collective-permute-start(f32[64,16,1]{2,1,0:T(8,128)S(1)} %get-tuple-element.28), channel_id=1, source_target_pairs={{0,32},{32,64},{64,96},{96,128},{128,160},{160,192},{192,224},{1,3... | collective-permute-start | bytes 12296 | tf_op jit(solution)/shard_map/ppermute | solution.py:21
  42.3 16.1 %collective-permute-start.4 = (f32[64,16,1]{2,1,0:T(8,128)S(1)}, f32[64,16,1]{2,1,0:T(8,128)S(1)}, u32[]{:S(2)}, u32[]{:S(2)}) collective-permute-start(f32[64,16,1]{2,1,0:T(8,128)S(1)} %get-tuple-element.29), channel_id=1, source_target_pairs={{32,0},{64,32},{96,64},{128,96},{160,128},{192,160},{224,192},{33,... | collective-permute-start | bytes 12296 | tf_op jit(solution)/shard_map/ppermute | solution.py:22
  58.9 17.5 %collective-permute-start.5 = (f32[64,1,130]{2,1,0:T(1,128)S(1)}, f32[64,1,130]{2,1,0:T(1,128)S(1)}, u32[]{:S(2)}, u32[]{:S(2)}) collective-permute-start(f32[64,1,130]{2,1,0:T(1,128)S(1)} %get-tuple-element.23), channel_id=1, source_target_pairs={{0,4},{4,8},{8,12},{12,16},{16,20},{20,24},{24,28},{1,5},{5,9},{9,... | collective-permute-start | bytes 99848 | tf_op jit(solution)/shard_map/ppermute | solution.py:21
  75.1 6.2 collective-permute-start.6
  82.2 1.1 copy-start.1
  176.7 13.8 %collective-permute-start.8 = (f32[64,16,128]{2,1,0:T(8,128)S(1)}, f32[64,16,128]{2,1,0:T(8,128)S(1)}, u32[]{:S(2)}, u32[]{:S(2)}) collective-permute-start(f32[64,16,128]{2,1,0:T(8,128)S(1)} %fusion.39), channel_id=1, source_target_pairs={{0,1},{1,2},{2,3},{3,0},{4,5},{5,6},{6,7},{7,4},{8,9},{9,10},{10,1... | collective-permute-start | bytes 1572872 | tf_op jit(solution)/shard_map/ppermute | solution.py:88
  177.4 15.1 %collective-permute-start.7 = (f32[64,16,128]{2,1,0:T(8,128)S(1)}, f32[64,16,128]{2,1,0:T(8,128)S(1)}, u32[]{:S(2)}, u32[]{:S(2)}) collective-permute-start(f32[64,16,128]{2,1,0:T(8,128)S(1)} %fusion.39), channel_id=1, source_target_pairs={{0,3},{1,0},{2,1},{3,2},{4,7},{5,4},{6,5},{7,6},{8,11},{9,8},{10,9... | collective-permute-start | bytes 1572872 | tf_op jit(solution)/shard_map/ppermute | solution.py:90
  190.4 13.6 %collective-permute-start.9 = (f32[64,16,128]{2,1,0:T(8,128)S(1)}, f32[64,16,128]{2,1,0:T(8,128)S(1)}, u32[]{:S(2)}, u32[]{:S(2)}) collective-permute-start(f32[64,16,128]{2,1,0:T(8,128)S(1)} %collective-permute-done.8), channel_id=1, source_target_pairs={{0,1},{1,2},{2,3},{3,0},{4,5},{5,6},{6,7},{7,4},{8,9},{9,10},{10,1... | collective-permute-start | bytes 1572872 | tf_op jit(solution)/shard_map/ppermute | solution.py:88
  191.8 12.9 %copy-start.9 = (f32[56,16,128]{2,1,0:T(8,128)S(1)}, f32[56,16,128]{2,1,0:T(8,128)}, u32[]{:S(2)}) copy-start(f32[56,16,128]{2,1,0:T(8,128)} %param.4) | copy-start | bytes 1376260
  208.8 258.0 %reduce-scatter.8.cloned.1.call-start = ((), (), s32[]{:S(2)}) async-start(), calls=%async_computation.5 | async-start | bytes 2621440 | tf_op jit(solution)/shard_map/reduce_scatter | solution.py:108
  209.1 2.8 collective-permute-start.10
  210.4 4.8 collective-permute-start.11
  215.7 3.6 collective-permute-start.12
  217.5 6.2 collective-permute-start.13
  224.5 1.2 copy-start.4
  315.3 1.1 copy-start.2
  324.5 14.4 %collective-permute-start.15 = (f32[64,16,128]{2,1,0:T(8,128)S(1)}, f32[64,16,128]{2,1,0:T(8,128)S(1)}, u32[]{:S(2)}, u32[]{:S(2)}) collective-permute-start(f32[64,16,128]{2,1,0:T(8,128)S(1)} %fusion.32), channel_id=1, source_target_pairs={{0,1},{1,2},{2,3},{3,0},{4,5},{5,6},{6,7},{7,4},{8,9},{9,10},{10,1... | collective-permute-start | bytes 1572872 | tf_op jit(solution)/shard_map/ppermute | solution.py:88
  326.4 15.3 %collective-permute-start.14 = (f32[64,16,128]{2,1,0:T(8,128)S(1)}, f32[64,16,128]{2,1,0:T(8,128)S(1)}, u32[]{:S(2)}, u32[]{:S(2)}) collective-permute-start(f32[64,16,128]{2,1,0:T(8,128)S(1)} %fusion.32), channel_id=1, source_target_pairs={{0,3},{1,0},{2,1},{3,2},{4,7},{5,4},{6,5},{7,6},{8,11},{9,8},{10,9... | collective-permute-start | bytes 1572872 | tf_op jit(solution)/shard_map/ppermute | solution.py:90
  338.9 14.0 %collective-permute-start.16 = (f32[64,16,128]{2,1,0:T(8,128)S(1)}, f32[64,16,128]{2,1,0:T(8,128)S(1)}, u32[]{:S(2)}, u32[]{:S(2)}) collective-permute-start(f32[64,16,128]{2,1,0:T(8,128)S(1)} %collective-permute-done.15), channel_id=1, source_target_pairs={{0,1},{1,2},{2,3},{3,0},{4,5},{5,6},{6,7},{7,4},{8,9},{9,10},{10,1... | collective-permute-start | bytes 1572872 | tf_op jit(solution)/shard_map/ppermute | solution.py:88
  341.0 12.6 %copy-start.10 = (f32[56,16,128]{2,1,0:T(8,128)S(1)}, f32[56,16,128]{2,1,0:T(8,128)}, u32[]{:S(2)}) copy-start(f32[56,16,128]{2,1,0:T(8,128)} %param.4) | copy-start | bytes 1376260
  357.8 145.2 %all-gather.2.cloned.1.call-start = ((), (), s32[]{:S(2)}) async-start(), calls=%async_computation.6 | async-start | bytes 2621440 | tf_op jit(solution)/shard_map/all_gather | solution.py:118
  358.0 2.8 collective-permute-start.17
  359.3 4.0 collective-permute-start.18
  363.3 8.0 %copy-start.5 = (f32[64,16,1]{2,1,0:T(8,128)}, f32[64,16,1]{2,1,0:T(8,128)S(1)}, u32[]{:S(2)}) copy-start(f32[64,16,1]{2,1,0:T(8,128)S(1)} %collective-permute-done.18) | copy-start | bytes 12292
  363.8 3.2 collective-permute-start.19
  365.1 6.2 collective-permute-start.20
  372.2 1.2 copy-start.3
  460.5 3.7 copy-start.6
  472.8 33.8 %copy-start.11 = (f32[56,16,128]{2,1,0:T(8,128)S(1)}, f32[56,16,128]{2,1,0:T(8,128)}, u32[]{:S(2)}) copy-start(f32[56,16,128]{2,1,0:T(8,128)} %param.4) | copy-start | bytes 1376260
  503.0 3.8 copy-start.7
Sparse Core Ops, SparseCore 0:
  39.9 34.2 reduce-scatter.3
  209.0 29.0 reduce-scatter.5
  357.9 28.8 reduce-scatter.7
  473.0 29.9 all-gather.1
